TPU v7x, 32 devices: a whole 2x2x4 slice. The times are simulated.
32 devices in a mesh: seq: 8 (over z, x), head: 4 (over y, core).
Axes of the slice: x: 2, y: 2, z: 4, core: 2. Of those that a mesh axis runs over, the one named last changes fastest.
Arguments:
- query_act: bfloat16 [10240, 5120], P('seq', 'head'), may hold values from -5.5 to 5.5
- key_act: bfloat16 [10240, 5120], P('seq', 'head'), may hold values from -5.5 to 5.5
- value_act: bfloat16 [10240, 5120], P('seq', 'head'), may hold values from -6 to 6
- block_lists: int32 [80, 26], P('seq'), may hold values from -1 to 79, as said below
- key_stride: int32 [4], replicated, may hold values from 1 to 8, as said below
- out_weight: bfloat16 [5120, 5120], P('head'), may hold values from -0.3125 to 0.3125
Outputs:
- layer_out: bfloat16 [10240, 5120], P('seq', 'head')
Inputs may be any that keep to these rules, and one draw needn't show every extreme that they name: `block_lists`: row i lists distinct key blocks: the 10 blocks of query block i's own frame and, for every frame at distance d of 1 to 3 on either side, max(1, 10 // 2**d) consecutive blocks of that frame; a slot holds -1 where that frame lies outside the clip. Slots stand in any order. `key_stride`: strides never fall as the distance grows; distance 0 has stride 1 and distance 3 has stride 8.
All inputs are finite; a program needn't handle non-finite values.
Results may differ from a plain program's by a relative error of at most 0.013.
Values may be sent and summed in bfloat16 or wider, within the bound.
No kernel may reach another device: no remote copies, remote signals or barrier semaphores. Data moves between devices by JAX's collectives and lax.ppermute only.
A program may use at most 192 MiB of HBM per device.

v0:
```python
import math

import jax
import jax.numpy as jnp
from jax import lax
from jax.sharding import PartitionSpec as P

HD = 128
BLK = 128
FRAME_BLK = 10
REACH = 3


def from_behind(shard, axis, by):
    peers = lax.axis_size(axis)
    pairs = [(i, i + by) for i in range(peers) if 0 <= i + by < peers]
    return lax.ppermute(shard, axis, pairs)


def band_window(kv_pair):
    blocks_here = kv_pair.shape[2] // BLK
    reach_dev = -(-(REACH * FRAME_BLK) // blocks_here)
    offsets = list(range(reach_dev, 0, -1)) + list(range(-1, -reach_dev - 1, -1))
    shifted = [from_behind(kv_pair, "seq", offset) for offset in offsets]
    pieces = shifted[:reach_dev] + [kv_pair] + shifted[reach_dev:]
    return (jnp.concatenate(pieces, axis=2), reach_dev)


def shards(query_act, key_act, value_act, block_lists, key_stride, out_weight):
    rows_here = query_act.shape[0]
    blocks_here = rows_here // BLK
    heads_here = query_act.shape[1] // HD
    score_scale = 1.0 / math.sqrt(HD)
    kv_pair = jnp.stack(
        [key_act.reshape(rows_here, heads_here, HD), value_act.reshape(rows_here, heads_here, HD)]
    )
    kv_pair = jnp.transpose(kv_pair, (0, 2, 1, 3))
    window, reach_dev = band_window(kv_pair)
    win_blocks = window.shape[2] // BLK
    window = window.reshape(2, heads_here, win_blocks, BLK, HD)
    seq_index = lax.axis_index("seq")
    first_block = (seq_index - reach_dev) * blocks_here
    query_blocks = seq_index * blocks_here + jnp.arange(blocks_here, dtype=jnp.int32)
    usable = block_lists >= 0
    slot_rows = jnp.where(usable, block_lists - first_block, 0)
    distance = jnp.abs(query_blocks[:, None] // FRAME_BLK - block_lists // FRAME_BLK)
    levels = jnp.arange(REACH + 1, dtype=jnp.int32)
    step_of = jnp.sum(
        jnp.where(distance[:, :, None] == levels[None, None, :], key_stride[None, None, :], 0),
        axis=2,
    )
    step_of = jnp.where(usable, step_of, 1)
    in_block = jnp.arange(BLK, dtype=jnp.int32)
    keep_key = usable[:, :, None] & (in_block[None, None, :] % step_of[:, :, None] == 0)
    per_step = math.gcd(blocks_here, 4)
    groups = blocks_here // per_step
    queries = jnp.transpose(
        query_act.reshape(groups, per_step, BLK, heads_here, HD), (0, 3, 1, 2, 4)
    )

    def attend(packet):
        group_q, group_slots, group_keep = packet
        picked = window[:, :, group_slots].reshape(2, heads_here, per_step, -1, HD)
        scores = (
            jnp.einsum("hgqd,hgkd->hgqk", group_q, picked[0], preferred_element_type=jnp.float32)
            * score_scale
        )
        kept_mask = group_keep[None, :, None, :]
        scores = jnp.where(kept_mask, scores, -1e30)
        row_max = jnp.max(scores, axis=3, keepdims=True)
        exps_kept = jnp.where(kept_mask, jnp.exp(scores - row_max), 0.0)
        row_total = jnp.sum(exps_kept, axis=3)
        weights = exps_kept.astype(jnp.bfloat16)
        combined = jnp.einsum(
            "hgqk,hgkd->hgqd", weights, picked[1], preferred_element_type=jnp.float32
        )
        combined = combined / row_total[:, :, :, None]
        return combined.astype(jnp.bfloat16)

    attended = lax.map(
        attend,
        (queries, slot_rows.reshape(groups, per_step, -1), keep_key.reshape(groups, per_step, -1)),
    )
    attended = jnp.transpose(attended, (0, 2, 3, 1, 4)).reshape(rows_here, heads_here * HD)
    partial_sum = jnp.dot(attended, out_weight, preferred_element_type=jnp.float32)
    layer_out = lax.psum_scatter(
        partial_sum.astype(jnp.bfloat16), "head", scatter_dimension=1, tiled=True
    )
    return layer_out


def solution(mesh):
    placed = (
        P("seq", "head"),
        P("seq", "head"),
        P("seq", "head"),
        P("seq", None),
        P(),
        P("head", None),
    )
    return jax.shard_map(
        shards, mesh=mesh, in_specs=placed, out_specs=P("seq", "head"), check_vma=False
    )
```

profile of v0, /device:TPU:16, one launch (start us, length us, event | category | flops | bytes accessed | tf_op | source)
XLA Modules:
  0.0 1509.2 jit_solution(5308184370320635636)
XLA Ops:
  6.5 4.0 copy.26
  10.6 5.6 copy.27
  16.2 5.3 maximum_bitcast_fusion
  21.4 4.4 collective-permute-start
  25.9 1.9 collective-permute-start.1
  27.8 1.9 collective-permute-start.2
  29.7 4.8 collective-permute-start.3
  34.5 5.6 collective-permute-start.4
  40.2 129.4 %collective-permute-done = bf16[2,10,1280,128]{2,3,1,0:T(8,128)(2,1)} collective-permute-done((bf16[2,10,1280,128]{2,3,1,0:T(8,128)(2,1)}, bf16[2,10,1280,128]{2,3,1,0:T(8,128)(2,1)}, u32[]{:S(2)}, u32[]{:S(2)}) %collective-permute-start) | collective-permute-done | bytes 6553632 | tf_op jit(solution)/shard_map/ppermute | solution.py:17
  169.5 1.9 collective-permute-start.5
  174.1 5.6 copy.25
  179.7 7.2 reshape.83
  186.8 6.1 compare_and_fusion
  192.9 6.2 constant_dynamic-update-slice_fusion.6
  199.1 240.8 %collective-permute-done.1 = bf16[2,10,1280,128]{2,3,1,0:T(8,128)(2,1)} collective-permute-done((bf16[2,10,1280,128]{2,3,1,0:T(8,128)(2,1)}, bf16[2,10,1280,128]{2,3,1,0:T(8,128)(2,1)}, u32[]{:S(2)}, u32[]{:S(2)}) %collective-permute-start.1) | collective-permute-done | bytes 6553632 | tf_op jit(solution)/shard_map/ppermute | solution.py:17
  439.9 6.4 constant_dynamic-update-slice_fusion.5
  446.2 143.5 %collective-permute-done.2 = bf16[2,10,1280,128]{2,3,1,0:T(8,128)(2,1)} collective-permute-done((bf16[2,10,1280,128]{2,3,1,0:T(8,128)(2,1)}, bf16[2,10,1280,128]{2,3,1,0:T(8,128)(2,1)}, u32[]{:S(2)}, u32[]{:S(2)}) %collective-permute-start.2) | collective-permute-done | bytes 6553632 | tf_op jit(solution)/shard_map/ppermute | solution.py:17
  589.7 6.4 constant_dynamic-update-slice_fusion.4
  596.1 3.5 constant_dynamic-update-slice_fusion.3
  599.6 6.4 constant_dynamic-update-slice_fusion.2
  606.0 6.4 constant_dynamic-update-slice_fusion.1
  612.5 114.8 %collective-permute-done.5 = bf16[2,10,1280,128]{2,3,1,0:T(8,128)(2,1)} collective-permute-done((bf16[2,10,1280,128]{2,3,1,0:T(8,128)(2,1)}, bf16[2,10,1280,128]{2,3,1,0:T(8,128)(2,1)}, u32[]{:S(2)}, u32[]{:S(2)}) %collective-permute-start.5) | collective-permute-done | bytes 6553632 | tf_op jit(solution)/shard_map/ppermute | solution.py:17
  727.2 6.4 constant_dynamic-update-slice_fusion
  733.6 59.3 %copy.28 = bf16[2,10,8960,128]{3,2,1,0:T(8,128)(2,1)} copy(bf16[2,10,8960,128]{2,3,1,0:T(8,128)(2,1)} %constant_dynamic-update-slice_fusion) | data formatting | bytes 91750400 | tf_op jit(solution)/shard_map/concatenate | solution.py:26
  792.9 568.4 %while.10 = (s32[]{:T(128)}, bf16[5,10,2,128,128]{4,3,2,1,0:T(8,128)(2,1)}, pred[5,2,3328]{2,1,0:T(4,128)(4,1)S(1)}, bf16[5,10,2,128,128]{3,2,0,4,1:T(2,128)(2,1...) while((s32[]{:T(128)}, bf16[5,10,2,128,128]{4,3,2,1,0:T(8,128)(2,1)}, ...), condition=%wide.region_4.5_spmd, body=%wide.region_1.4_spmd.sunk | while | flops 4413854208 | bytes 276608320 | solution.py:80
  793.6 25.2 %gather_fusion = bf16[52,2,10,128,128]{4,3,2,1,0:T(8,128)(2,1)} fusion(bf16[2,10,70,128,128]{4,3,2,1,0:T(8,128)(2,1)} %get-tuple-element.143, s32[1024]{0:T(1024)S(1)} %pad_clamp_fusion.2), kind=kCustom, calls=%fused_computation.clone.1 | custom fusion | bytes 68157648 | tf_op jit(solution)/shard_map/while/body/eval_jaxpr/gather | solution.py:63
  818.8 23.1 %copy.36 = bf16[2,26,2,10,128,128]{5,4,1,0,3,2:T(8,128)(2,1)} copy(bf16[2,26,2,10,128,128]{5,4,3,2,1,0:T(8,128)(2,1)} %bitcast.73) | data formatting | bytes 68157440 | tf_op jit(solution)/shard_map/while/body/eval_jaxpr/gather | solution.py:63
  841.9 28.0 %fusion.52 = (bf16[1,10,2,26,128,128]{5,4,3,2,1,0:T(8,128)(2,1)}, bf16[1,10,2,26,128,128]{5,4,3,2,1,0:T(8,128)(2,1)}) fusion(bf16[2,10,2,26,128,128]{5,4,3,2,1,0:T(8,128)(2,1)} %bitcast.72), kind=kLoop, calls=%fused_computation.49.clone.1 | loop fusion | bytes 68157440 | tf_op jit(solution)/shard_map/while/body/eval_jaxpr/slice | solution.py:65
  869.9 1.6 constant_dynamic-slice_fusion.2
  871.6 0.9 copy.37
  872.5 17.9 %fusion.53 = (f32[10,2,128]{2,1,0:T(2,128)S(1)}, bf16[10,2,128,3328]{3,2,1,0:T(8,128)(2,1)}) fusion(pred[2,3328]{1,0:T(4,128)(4,1)S(1)} %dynamic-slice_bitcast_fusion.2, bf16[10,2,3328,128]{3,2,1,0:T(8,128)(2,1)} %bitcast.76, bf16[1,10,2,128,128]{4,3,2,1,0:T(8,128)(2,1)S(1)} %copy.37), kind=kOutput, calls=%fused_computation.50.clone.1 | convolution fusion | flops 2232159488 | bytes 34750976 | tf_op jit(solution)/shard_map/while/body/eval_jaxpr/sub | solution.py:71
  890.4 16.1 %fusion.54 = bf16[5,10,2,128,128]{4,3,2,1,0:T(8,128)(2,1)} fusion(bf16[5,10,2,128,128]{4,3,2,1,0:T(8,128)(2,1)} %get-tuple-element.132, s32[]{:T(128)} %get-tuple-element.131, bf16[10,2,3328,128]{3,2,1,0:T(8,128)(2,1)} %bitcast.75, bf16[10,2,128,3328]{3,2,1,0:T(8,128)(2,1)} %get-tuple-element.122, f32[10,2,128]{2,1,0:T(2,128)S(1)} %get-tuple-element.123), kind=kOutput, calls=%fused_computation.14.clone.1 | convolution fusion | flops 2181693440 | bytes 34744832 | tf_op jit(solution)/shard_map/while/body/eval_jaxpr/hgqk,hgkd->hgqd/dot_general | solution.py:74
  907.3 25.1 %gather_fusion = bf16[52,2,10,128,128]{4,3,2,1,0:T(8,128)(2,1)} fusion(bf16[2,10,70,128,128]{4,3,2,1,0:T(8,128)(2,1)} %get-tuple-element.143, s32[1024]{0:T(1024)S(1)} %pad_clamp_fusion.2), kind=kCustom, calls=%fused_computation.clone.1 | custom fusion | bytes 68157648 | tf_op jit(solution)/shard_map/while/body/eval_jaxpr/gather | solution.py:63
  932.5 23.1 %copy.36 = bf16[2,26,2,10,128,128]{5,4,1,0,3,2:T(8,128)(2,1)} copy(bf16[2,26,2,10,128,128]{5,4,3,2,1,0:T(8,128)(2,1)} %bitcast.73) | data formatting | bytes 68157440 | tf_op jit(solution)/shard_map/while/body/eval_jaxpr/gather | solution.py:63
  955.6 28.0 %fusion.52 = (bf16[1,10,2,26,128,128]{5,4,3,2,1,0:T(8,128)(2,1)}, bf16[1,10,2,26,128,128]{5,4,3,2,1,0:T(8,128)(2,1)}) fusion(bf16[2,10,2,26,128,128]{5,4,3,2,1,0:T(8,128)(2,1)} %bitcast.72), kind=kLoop, calls=%fused_computation.49.clone.1 | loop fusion | bytes 68157440 | tf_op jit(solution)/shard_map/while/body/eval_jaxpr/slice | solution.py:65
  983.6 1.6 constant_dynamic-slice_fusion.2
  985.2 0.9 copy.37
  986.2 17.9 %fusion.53 = (f32[10,2,128]{2,1,0:T(2,128)S(1)}, bf16[10,2,128,3328]{3,2,1,0:T(8,128)(2,1)}) fusion(pred[2,3328]{1,0:T(4,128)(4,1)S(1)} %dynamic-slice_bitcast_fusion.2, bf16[10,2,3328,128]{3,2,1,0:T(8,128)(2,1)} %bitcast.76, bf16[1,10,2,128,128]{4,3,2,1,0:T(8,128)(2,1)S(1)} %copy.37), kind=kOutput, calls=%fused_computation.50.clone.1 | convolution fusion | flops 2232159488 | bytes 34750976 | tf_op jit(solution)/shard_map/while/body/eval_jaxpr/sub | solution.py:71
  1004.1 16.1 %fusion.54 = bf16[5,10,2,128,128]{4,3,2,1,0:T(8,128)(2,1)} fusion(bf16[5,10,2,128,128]{4,3,2,1,0:T(8,128)(2,1)} %get-tuple-element.132, s32[]{:T(128)} %get-tuple-element.131, bf16[10,2,3328,128]{3,2,1,0:T(8,128)(2,1)} %bitcast.75, bf16[10,2,128,3328]{3,2,1,0:T(8,128)(2,1)} %get-tuple-element.122, f32[10,2,128]{2,1,0:T(2,128)S(1)} %get-tuple-element.123), kind=kOutput, calls=%fused_computation.14.clone.1 | convolution fusion | flops 2181693440 | bytes 34744832 | tf_op jit(solution)/shard_map/while/body/eval_jaxpr/hgqk,hgkd->hgqd/dot_general | solution.py:74
  1021.0 25.1 %gather_fusion = bf16[52,2,10,128,128]{4,3,2,1,0:T(8,128)(2,1)} fusion(bf16[2,10,70,128,128]{4,3,2,1,0:T(8,128)(2,1)} %get-tuple-element.143, s32[1024]{0:T(1024)S(1)} %pad_clamp_fusion.2), kind=kCustom, calls=%fused_computation.clone.1 | custom fusion | bytes 68157648 | tf_op jit(solution)/shard_map/while/body/eval_jaxpr/gather | solution.py:63
  1046.1 23.1 %copy.36 = bf16[2,26,2,10,128,128]{5,4,1,0,3,2:T(8,128)(2,1)} copy(bf16[2,26,2,10,128,128]{5,4,3,2,1,0:T(8,128)(2,1)} %bitcast.73) | data formatting | bytes 68157440 | tf_op jit(solution)/shard_map/while/body/eval_jaxpr/gather | solution.py:63
  1069.2 28.0 %fusion.52 = (bf16[1,10,2,26,128,128]{5,4,3,2,1,0:T(8,128)(2,1)}, bf16[1,10,2,26,128,128]{5,4,3,2,1,0:T(8,128)(2,1)}) fusion(bf16[2,10,2,26,128,128]{5,4,3,2,1,0:T(8,128)(2,1)} %bitcast.72), kind=kLoop, calls=%fused_computation.49.clone.1 | loop fusion | bytes 68157440 | tf_op jit(solution)/shard_map/while/body/eval_jaxpr/slice | solution.py:65
  1097.3 1.6 constant_dynamic-slice_fusion.2
  1098.9 0.9 copy.37
  1099.9 17.9 %fusion.53 = (f32[10,2,128]{2,1,0:T(2,128)S(1)}, bf16[10,2,128,3328]{3,2,1,0:T(8,128)(2,1)}) fusion(pred[2,3328]{1,0:T(4,128)(4,1)S(1)} %dynamic-slice_bitcast_fusion.2, bf16[10,2,3328,128]{3,2,1,0:T(8,128)(2,1)} %bitcast.76, bf16[1,10,2,128,128]{4,3,2,1,0:T(8,128)(2,1)S(1)} %copy.37), kind=kOutput, calls=%fused_computation.50.clone.1 | convolution fusion | flops 2232159488 | bytes 34750976 | tf_op jit(solution)/shard_map/while/body/eval_jaxpr/sub | solution.py:71
  1117.8 16.1 %fusion.54 = bf16[5,10,2,128,128]{4,3,2,1,0:T(8,128)(2,1)} fusion(bf16[5,10,2,128,128]{4,3,2,1,0:T(8,128)(2,1)} %get-tuple-element.132, s32[]{:T(128)} %get-tuple-element.131, bf16[10,2,3328,128]{3,2,1,0:T(8,128)(2,1)} %bitcast.75, bf16[10,2,128,3328]{3,2,1,0:T(8,128)(2,1)} %get-tuple-element.122, f32[10,2,128]{2,1,0:T(2,128)S(1)} %get-tuple-element.123), kind=kOutput, calls=%fused_computation.14.clone.1 | convolution fusion | flops 2181693440 | bytes 34744832 | tf_op jit(solution)/shard_map/while/body/eval_jaxpr/hgqk,hgkd->hgqd/dot_general | solution.py:74
  1134.7 25.1 %gather_fusion = bf16[52,2,10,128,128]{4,3,2,1,0:T(8,128)(2,1)} fusion(bf16[2,10,70,128,128]{4,3,2,1,0:T(8,128)(2,1)} %get-tuple-element.143, s32[1024]{0:T(1024)S(1)} %pad_clamp_fusion.2), kind=kCustom, calls=%fused_computation.clone.1 | custom fusion | bytes 68157648 | tf_op jit(solution)/shard_map/while/body/eval_jaxpr/gather | solution.py:63
  1159.8 23.1 %copy.36 = bf16[2,26,2,10,128,128]{5,4,1,0,3,2:T(8,128)(2,1)} copy(bf16[2,26,2,10,128,128]{5,4,3,2,1,0:T(8,128)(2,1)} %bitcast.73) | data formatting | bytes 68157440 | tf_op jit(solution)/shard_map/while/body/eval_jaxpr/gather | solution.py:63
  1182.9 28.0 %fusion.52 = (bf16[1,10,2,26,128,128]{5,4,3,2,1,0:T(8,128)(2,1)}, bf16[1,10,2,26,128,128]{5,4,3,2,1,0:T(8,128)(2,1)}) fusion(bf16[2,10,2,26,128,128]{5,4,3,2,1,0:T(8,128)(2,1)} %bitcast.72), kind=kLoop, calls=%fused_computation.49.clone.1 | loop fusion | bytes 68157440 | tf_op jit(solution)/shard_map/while/body/eval_jaxpr/slice | solution.py:65
  1210.9 1.6 constant_dynamic-slice_fusion.2
  1212.6 0.9 copy.37
  1213.5 17.9 %fusion.53 = (f32[10,2,128]{2,1,0:T(2,128)S(1)}, bf16[10,2,128,3328]{3,2,1,0:T(8,128)(2,1)}) fusion(pred[2,3328]{1,0:T(4,128)(4,1)S(1)} %dynamic-slice_bitcast_fusion.2, bf16[10,2,3328,128]{3,2,1,0:T(8,128)(2,1)} %bitcast.76, bf16[1,10,2,128,128]{4,3,2,1,0:T(8,128)(2,1)S(1)} %copy.37), kind=kOutput, calls=%fused_computation.50.clone.1 | convolution fusion | flops 2232159488 | bytes 34750976 | tf_op jit(solution)/shard_map/while/body/eval_jaxpr/sub | solution.py:71
  1231.4 16.1 %fusion.54 = bf16[5,10,2,128,128]{4,3,2,1,0:T(8,128)(2,1)} fusion(bf16[5,10,2,128,128]{4,3,2,1,0:T(8,128)(2,1)} %get-tuple-element.132, s32[]{:T(128)} %get-tuple-element.131, bf16[10,2,3328,128]{3,2,1,0:T(8,128)(2,1)} %bitcast.75, bf16[10,2,128,3328]{3,2,1,0:T(8,128)(2,1)} %get-tuple-element.122, f32[10,2,128]{2,1,0:T(2,128)S(1)} %get-tuple-element.123), kind=kOutput, calls=%fused_computation.14.clone.1 | convolution fusion | flops 2181693440 | bytes 34744832 | tf_op jit(solution)/shard_map/while/body/eval_jaxpr/hgqk,hgkd->hgqd/dot_general | solution.py:74
  1248.3 25.1 %gather_fusion = bf16[52,2,10,128,128]{4,3,2,1,0:T(8,128)(2,1)} fusion(bf16[2,10,70,128,128]{4,3,2,1,0:T(8,128)(2,1)} %get-tuple-element.143, s32[1024]{0:T(1024)S(1)} %pad_clamp_fusion.2), kind=kCustom, calls=%fused_computation.clone.1 | custom fusion | bytes 68157648 | tf_op jit(solution)/shard_map/while/body/eval_jaxpr/gather | solution.py:63
  1273.5 23.1 %copy.36 = bf16[2,26,2,10,128,128]{5,4,1,0,3,2:T(8,128)(2,1)} copy(bf16[2,26,2,10,128,128]{5,4,3,2,1,0:T(8,128)(2,1)} %bitcast.73) | data formatting | bytes 68157440 | tf_op jit(solution)/shard_map/while/body/eval_jaxpr/gather | solution.py:63
  1296.6 28.0 %fusion.52 = (bf16[1,10,2,26,128,128]{5,4,3,2,1,0:T(8,128)(2,1)}, bf16[1,10,2,26,128,128]{5,4,3,2,1,0:T(8,128)(2,1)}) fusion(bf16[2,10,2,26,128,128]{5,4,3,2,1,0:T(8,128)(2,1)} %bitcast.72), kind=kLoop, calls=%fused_computation.49.clone.1 | loop fusion | bytes 68157440 | tf_op jit(solution)/shard_map/while/body/eval_jaxpr/slice | solution.py:65
  1324.6 1.6 constant_dynamic-slice_fusion.2
  1326.2 0.9 copy.37
  1327.2 17.9 %fusion.53 = (f32[10,2,128]{2,1,0:T(2,128)S(1)}, bf16[10,2,128,3328]{3,2,1,0:T(8,128)(2,1)}) fusion(pred[2,3328]{1,0:T(4,128)(4,1)S(1)} %dynamic-slice_bitcast_fusion.2, bf16[10,2,3328,128]{3,2,1,0:T(8,128)(2,1)} %bitcast.76, bf16[1,10,2,128,128]{4,3,2,1,0:T(8,128)(2,1)S(1)} %copy.37), kind=kOutput, calls=%fused_computation.50.clone.1 | convolution fusion | flops 2232159488 | bytes 34750976 | tf_op jit(solution)/shard_map/while/body/eval_jaxpr/sub | solution.py:71
  1345.1 16.1 %fusion.54 = bf16[5,10,2,128,128]{4,3,2,1,0:T(8,128)(2,1)} fusion(bf16[5,10,2,128,128]{4,3,2,1,0:T(8,128)(2,1)} %get-tuple-element.132, s32[]{:T(128)} %get-tuple-element.131, bf16[10,2,3328,128]{3,2,1,0:T(8,128)(2,1)} %bitcast.75, bf16[10,2,128,3328]{3,2,1,0:T(8,128)(2,1)} %get-tuple-element.122, f32[10,2,128]{2,1,0:T(2,128)S(1)} %get-tuple-element.123), kind=kOutput, calls=%fused_computation.14.clone.1 | convolution fusion | flops 2181693440 | bytes 34744832 | tf_op jit(solution)/shard_map/while/body/eval_jaxpr/hgqk,hgkd->hgqd/dot_general | solution.py:74
  1361.3 10.1 copy.30
  1371.4 3.4 reshape.86
  1374.7 24.1 %convolution_convert_fusion = bf16[1280,5120]{1,0:T(8,128)(2,1)} fusion(bf16[1280,1280]{0,1:T(8,128)(2,1)} %reshape.86, bf16[1280,5120]{1,0:T(8,128)(2,1)} %param.13), kind=kOutput, calls=%fused_computation.24 | convolution fusion | flops 16783769600 | bytes 29491200 | tf_op jit(solution)/shard_map/dot_general | solution.py:85
  1398.9 103.5 %reduce-scatter.2.cloned.1.call-done = bf16[1280,1280]{1,0:T(8,128)(2,1)} async-done(((bf16[1280,5120]{1,0:T(8,128)(2,1)}), bf16[1280,1280]{1,0:T(8,128)(2,1)}) %reduce-scatter.2.cloned.1.call-update) | async-done | bytes 3276816 | tf_op jit(solution)/shard_map/reduce_scatter | solution.py:86
  (45 shorter events, 6.5 us)
Async XLA Ops:
  6.5 165.0 %copy-start.2 = (s32[10,26]{1,0:T(8,128)S(1)}, s32[10,26]{1,0:T(8,128)}, u32[]{:S(2)}) copy-start(s32[10,26]{1,0:T(8,128)} %param.11) | copy-start | bytes 3124
  6.5 165.1 %copy-start.3 = (s32[4]{0:T(128)S(1)}, s32[4]{0:T(128)}, u32[]{:S(2)}) copy-start(s32[4]{0:T(128)} %param.12) | copy-start | bytes 52
  6.5 1495.8 %reduce-scatter.2.cloned.1.call-start = ((), (), s32[]{:S(2)}) async-start(), calls=%async_computation.1 | async-start | bytes 16384000 | tf_op jit(solution)/shard_map/reduce_scatter | solution.py:86
  21.4 148.1 %collective-permute-start = (bf16[2,10,1280,128]{2,3,1,0:T(8,128)(2,1)}, bf16[2,10,1280,128]{2,3,1,0:T(8,128)(2,1)}, u32[]{:S(2)}, u32[]{:S(2)}) collective-permute-start(bf16[2,10,1280,128]{2,3,1,0:T(8,128)(2,1)} %maximum_bitcast_fusion), channel_id=1, source_target_pairs={{0,12},{4,16},{8,20},{12,24},{16,28},{1,13},{5,17},{9,21},{13,25},... | collective-permute-start | bytes 19660808 | tf_op jit(solution)/shard_map/ppermute | solution.py:17
  25.9 414.0 %collective-permute-start.1 = (bf16[2,10,1280,128]{2,3,1,0:T(8,128)(2,1)}, bf16[2,10,1280,128]{2,3,1,0:T(8,128)(2,1)}, u32[]{:S(2)}, u32[]{:S(2)}) collective-permute-start(bf16[2,10,1280,128]{2,3,1,0:T(8,128)(2,1)} %maximum_bitcast_fusion), channel_id=1, source_target_pairs={{0,8},{4,12},{8,16},{12,20},{16,24},{20,28},{1,9},{5,13},{9,17},{1... | collective-permute-start | bytes 19660808 | tf_op jit(solution)/shard_map/ppermute | solution.py:17
  27.8 562.0 %collective-permute-start.2 = (bf16[2,10,1280,128]{2,3,1,0:T(8,128)(2,1)}, bf16[2,10,1280,128]{2,3,1,0:T(8,128)(2,1)}, u32[]{:S(2)}, u32[]{:S(2)}) collective-permute-start(bf16[2,10,1280,128]{2,3,1,0:T(8,128)(2,1)} %maximum_bitcast_fusion), channel_id=1, source_target_pairs={{0,4},{4,8},{8,12},{12,16},{16,20},{20,24},{24,28},{1,5},{5,9},{9,... | collective-permute-start | bytes 19660808 | tf_op jit(solution)/shard_map/ppermute | solution.py:17
  29.7 569.9 %collective-permute-start.3 = (bf16[2,10,1280,128]{2,3,1,0:T(8,128)(2,1)}, bf16[2,10,1280,128]{2,3,1,0:T(8,128)(2,1)}, u32[]{:S(2)}, u32[]{:S(2)}) collective-permute-start(bf16[2,10,1280,128]{2,3,1,0:T(8,128)(2,1)} %maximum_bitcast_fusion), channel_id=1, source_target_pairs={{4,0},{8,4},{12,8},{16,12},{20,16},{24,20},{28,24},{5,1},{9,5},{13... | collective-permute-start | bytes 19660808 | tf_op jit(solution)/shard_map/ppermute | solution.py:17
  34.5 571.5 %collective-permute-start.4 = (bf16[2,10,1280,128]{2,3,1,0:T(8,128)(2,1)}, bf16[2,10,1280,128]{2,3,1,0:T(8,128)(2,1)}, u32[]{:S(2)}, u32[]{:S(2)}) collective-permute-start(bf16[2,10,1280,128]{2,3,1,0:T(8,128)(2,1)} %maximum_bitcast_fusion), channel_id=1, source_target_pairs={{8,0},{12,4},{16,8},{20,12},{24,16},{28,20},{9,1},{13,5},{17,9},{2... | collective-permute-start | bytes 19660808 | tf_op jit(solution)/shard_map/ppermute | solution.py:17
  169.5 557.7 %collective-permute-start.5 = (bf16[2,10,1280,128]{2,3,1,0:T(8,128)(2,1)}, bf16[2,10,1280,128]{2,3,1,0:T(8,128)(2,1)}, u32[]{:S(2)}, u32[]{:S(2)}) collective-permute-start(bf16[2,10,1280,128]{2,3,1,0:T(8,128)(2,1)} %maximum_bitcast_fusion), channel_id=1, source_target_pairs={{12,0},{16,4},{20,8},{24,12},{28,16},{13,1},{17,5},{21,9},{25,13},... | collective-permute-start | bytes 19660808 | tf_op jit(solution)/shard_map/ppermute | solution.py:17
  172.5 14.3 copy-start.1
  199.1 397.0 %copy-start = (bf16[1280,1280]{0,1:T(8,128)(2,1)S(1)}, bf16[1280,1280]{0,1:T(8,128)(2,1)}, u32[]{:S(2)}) copy-start(bf16[1280,1280]{0,1:T(8,128)(2,1)} %copy.27) | copy-start | bytes 9830404
Sparse Core Ops, SparseCore 0:
  1399.0 103.3 reduce-scatter.1
where the time goes:
time: 1510 us
  waiting for transfers between devices  732 us (48%)
  local copies, waits for them, and re-layouts  530 us (35%)
  matrix products  194 us (13%)
  starting transfers between devices  20.6 us (1%)
  other arithmetic  18.4 us (1%)
    ppermute x6, waiting for transfers between devices, from_behind(): return lax.ppermute(shard, axis, pairs)  628 us
    gather x10, local copies, waits for them, and re-layouts, attend(): picked = window[:, :, group_slots].reshape(2, heads_here, per_step, -1, HD)  241 us
    slice x5, local copies, waits for them, and re-layouts, attend(): picked[0]  140 us
    reduce_scatter x1, waiting for transfers between devices, shards(): lax.psum_scatter(partial_sum.astype(jnp.bfloat16), 'head', scatter_dimens...  103 us
    sub x5, matrix products, attend(): exps_kept = jnp.where(kept_mask, jnp.exp(scores - row_max), 0.0)  89.6 us
    dot_general x5, matrix products, attend(): jnp.einsum('hgqk,hgkd->hgqd', weights, picked[1], preferred_element_type=...  80.6 us
    concatenate x2, local copies, waits for them, and re-layouts, band_window(): return (jnp.concatenate(pieces, axis=2), reach_dev)  65.7 us
    unnamed x16, local copies, waits for them, and re-layouts  47 us
  transfers between devices with their start and end apart: 7, of which 5 were waited for; matrix products, arithmetic and copies ran while one was open for 4% of the time, Pallas kernels for 0%

commit v1 on v0

v1 whole, which is shorter than its diff:
```python
import functools
import math

import jax
import jax.numpy as jnp
from jax import lax
from jax.experimental import pallas as pl
from jax.experimental.pallas import tpu as pltpu
from jax.sharding import PartitionSpec as P

HD = 128
BLK = 128
FRAME_BLK = 10
REACH = 3
FAR_STRIDE = 8


def from_behind(shard, axis, by):
    peers = lax.axis_size(axis)
    pairs = [(i, i + by) for i in range(peers) if 0 <= i + by < peers]
    return lax.ppermute(shard, axis, pairs)


def spread_far(compact, rows):
    width = compact.shape[-1]
    grown = jnp.pad(compact.reshape(rows // FAR_STRIDE, 1, width), ((0, 0), (0, FAR_STRIDE - 1), (0, 0)))
    return grown.reshape(rows, width)


def band_window(act, reach_dev):
    rows = act.shape[0]
    pieces = []
    for offset in range(reach_dev, 0, -1):
        if offset == REACH:
            far = from_behind(act[::FAR_STRIDE], "seq", offset)
            pieces.append(spread_far(far, rows))
        else:
            pieces.append(from_behind(act, "seq", offset))
    pieces.append(act)
    for offset in range(1, reach_dev + 1):
        if offset == REACH:
            far = from_behind(act[::FAR_STRIDE], "seq", -offset)
            pieces.append(spread_far(far, rows))
        else:
            pieces.append(from_behind(act, "seq", -offset))
    return jnp.concatenate(pieces, axis=0)


def attend_kernel(rows_ref, q_ref, k_ref, v_ref, keep_ref, o_ref, m_sc, l_sc, acc_sc, *, heads, nslot, scale):
    i = pl.program_id(0)
    s = pl.program_id(1)

    @pl.when(s == 0)
    def _():
        m_sc[...] = jnp.full(m_sc.shape, -jnp.inf, jnp.float32)
        l_sc[...] = jnp.zeros(l_sc.shape, jnp.float32)
        acc_sc[...] = jnp.zeros(acc_sc.shape, jnp.float32)

    @pl.when(rows_ref[1, i * nslot + s] > 0)
    def _():
        keep = keep_ref[0] > 0.0
        for h in range(heads):
            cols = pl.ds(h * HD, HD)
            qh = q_ref[:, cols]
            kh = k_ref[:, cols]
            sc = lax.dot_general(qh, kh, (((1,), (1,)), ((), ())), preferred_element_type=jnp.float32)
            sc = jnp.where(keep, sc * scale, -jnp.inf)
            m_prev = m_sc[h]
            m_new = jnp.maximum(m_prev, jnp.max(sc, axis=1, keepdims=True))
            alpha = jnp.exp(m_prev - m_new)
            p = jnp.exp(sc - m_new)
            l_sc[h] = alpha * l_sc[h] + jnp.sum(p, axis=1, keepdims=True)
            pv = jnp.dot(p.astype(jnp.bfloat16), v_ref[:, cols], preferred_element_type=jnp.float32)
            acc_sc[:, cols] = alpha * acc_sc[:, cols] + pv
            m_sc[h] = m_new

    @pl.when(s == nslot - 1)
    def _():
        for h in range(heads):
            cols = pl.ds(h * HD, HD)
            o_ref[:, cols] = (acc_sc[:, cols] / l_sc[h]).astype(o_ref.dtype)


def attend(query, kwin, vwin, rows, live, keep):
    nq = query.shape[0] // BLK
    nslot = rows.shape[1]
    width = query.shape[1]
    heads = width // HD
    table = jnp.stack([rows.reshape(-1), live.reshape(-1)]).astype(jnp.int32)
    kernel = functools.partial(attend_kernel, heads=heads, nslot=nslot, scale=1.0 / math.sqrt(HD))
    q_spec = pl.BlockSpec((BLK, width), lambda i, s, t: (i, 0))
    kv_spec = pl.BlockSpec((BLK, width), lambda i, s, t: (t[0, i * nslot + s], 0))
    keep_spec = pl.BlockSpec((1, 1, BLK), lambda i, s, t: (i * nslot + s, 0, 0))
    return pl.pallas_call(
        kernel,
        out_shape=jax.ShapeDtypeStruct(query.shape, jnp.bfloat16),
        grid_spec=pltpu.PrefetchScalarGridSpec(
            num_scalar_prefetch=1,
            grid=(nq, nslot),
            in_specs=[q_spec, kv_spec, kv_spec, keep_spec],
            out_specs=pl.BlockSpec((BLK, width), lambda i, s, t: (i, 0)),
            scratch_shapes=[
                pltpu.VMEM((heads, BLK, 1), jnp.float32),
                pltpu.VMEM((heads, BLK, 1), jnp.float32),
                pltpu.VMEM((BLK, width), jnp.float32),
            ],
        ),
        compiler_params=pltpu.CompilerParams(dimension_semantics=("arbitrary", "arbitrary")),
        cost_estimate=pl.CostEstimate(
            flops=4 * query.shape[0] * nslot * BLK * width,
            transcendentals=query.shape[0] * nslot * BLK * heads,
            bytes_accessed=2 * nq * nslot * BLK * width * 2 + 2 * query.size * 2,
        ),
    )(table, query, kwin, vwin, keep.reshape(-1, 1, BLK))


def halving_scatter(partial_f32, axis):
    n = lax.axis_size(axis)
    me = lax.axis_index(axis)
    bits = n.bit_length() - 1
    rows, total = partial_f32.shape
    group = total // n
    held = partial_f32.astype(jnp.bfloat16).astype(jnp.float32)
    held = held.reshape((rows,) + (2,) * bits + (group,))
    for b in range(bits):
        dim = held.ndim - 2
        mine = (me >> b) & 1
        keep = lax.dynamic_index_in_dim(held, mine, axis=dim, keepdims=False)
        send = lax.dynamic_index_in_dim(held, 1 - mine, axis=dim, keepdims=False)
        pairs = [(i, i ^ (1 << b)) for i in range(n)]
        got = lax.ppermute(send.astype(jnp.bfloat16), axis, pairs)
        held = keep + got.astype(jnp.float32)
    return held.reshape(rows, group).astype(jnp.bfloat16)


def shards(query_act, key_act, value_act, block_lists, key_stride, out_weight):
    rows_here = query_act.shape[0]
    blocks_here = rows_here // BLK
    assert blocks_here == FRAME_BLK
    reach_dev = REACH
    kwin = band_window(key_act, reach_dev)
    vwin = band_window(value_act, reach_dev)

    seq_index = lax.axis_index("seq")
    first_block = (seq_index - reach_dev) * blocks_here
    query_blocks = seq_index * blocks_here + jnp.arange(blocks_here, dtype=jnp.int32)
    listed = -jnp.sort(-block_lists, axis=1)
    usable = listed >= 0
    slot_rows = listed - first_block
    last_row = jnp.min(jnp.where(usable, slot_rows, 1 << 20), axis=1, keepdims=True)
    slot_rows = jnp.where(usable, slot_rows, last_row)
    distance = jnp.abs(query_blocks[:, None] // FRAME_BLK - listed // FRAME_BLK)
    levels = jnp.arange(REACH + 1, dtype=jnp.int32)
    step_of = jnp.sum(
        jnp.where(distance[:, :, None] == levels[None, None, :], key_stride[None, None, :], 0),
        axis=2,
    )
    step_of = jnp.where(usable, step_of, 1)
    in_block = jnp.arange(BLK, dtype=jnp.int32)
    keep_key = usable[:, :, None] & (in_block[None, None, :] % step_of[:, :, None] == 0)

    attended = attend(
        query_act, kwin, vwin, slot_rows, usable.astype(jnp.int32), keep_key.astype(jnp.float32)
    )
    partial_sum = jnp.dot(attended, out_weight, preferred_element_type=jnp.float32)
    return halving_scatter(partial_sum, "head")


def solution(mesh):
    placed = (
        P("seq", "head"),
        P("seq", "head"),
        P("seq", "head"),
        P("seq", None),
        P(),
        P("head", None),
    )
    return jax.shard_map(
        shards, mesh=mesh, in_specs=placed, out_specs=P("seq", "head"), check_vma=False
    )
```

time: 1510 us -> 1520 us (level)
  Pallas kernels: 0 us -> 862 us
  local copies, waits for them, and re-layouts: 530 us -> 125 us
  waiting for transfers between devices: 732 us -> 432 us
  matrix products: 194 us -> 23.4 us
  starting transfers between devices: 20.6 us -> 44.2 us
    pallas_call x0 -> x1, Pallas kernels: none -> 862 us  [attend(): pl.pallas_call(kernel, out_shape=jax.ShapeDtypeStruct(query.shape, jnp.bf...]
    ppermute x6 -> x12, waiting for transfers between devices: 628 us -> 360 us  [from_behind(): return lax.ppermute(shard, axis, pairs)]
    gather x10 -> x0, local copies, waits for them, and re-layouts: 241 us -> none  [attend(): picked = window[:, :, group_slots].reshape(2, heads_here, per_step, -1, HD)]
    slice x5 -> x2, local copies, waits for them, and re-layouts: 140 us -> 10.6 us  [band_window(): far = from_behind(act[::FAR_STRIDE], 'seq', offset)]
    reduce_scatter x1 -> x0, waiting for transfers between devices: 103 us -> none  [shards(): lax.psum_scatter(partial_sum.astype(jnp.bfloat16), 'head', scatter_dimens...]
    sub x5 -> x0, matrix products: 89.6 us -> none  [attend(): exps_kept = jnp.where(kept_mask, jnp.exp(scores - row_max), 0.0)]
    dot_general x5 -> x0, matrix products: 80.6 us -> none  [attend(): jnp.einsum('hgqk,hgkd->hgqd', weights, picked[1], preferred_element_type=...]
    ppermute x0 -> x2, waiting for transfers between devices: none -> 72 us  [halving_scatter(): got = lax.ppermute(send.astype(jnp.bfloat16), axis, pairs)]
  transfers between devices with their start and end apart: 7 -> 14, of which waited for: 5 -> 6; matrix products, arithmetic and copies ran while one was open for 4% -> 5% of each run, Pallas kernels for 0% -> 0%
where the time goes in v1:
time: 1520 us
  Pallas kernels  862 us (57%)
  waiting for transfers between devices  432 us (28%)
  local copies, waits for them, and re-layouts  125 us (8%)
  starting transfers between devices  44.2 us (3%)
  other arithmetic  28.4 us (2%)
  matrix products  23.4 us (2%)
    pallas_call x1, Pallas kernels, attend(): pl.pallas_call(kernel, out_shape=jax.ShapeDtypeStruct(query.shape, jnp.bf...  862 us
    ppermute x12, waiting for transfers between devices, from_behind(): return lax.ppermute(shard, axis, pairs)  360 us
    ppermute x2, waiting for transfers between devices, halving_scatter(): got = lax.ppermute(send.astype(jnp.bfloat16), axis, pairs)  72 us
    unnamed x21, local copies, waits for them, and re-layouts  42.9 us
    ppermute x12, starting transfers between devices, from_behind(): return lax.ppermute(shard, axis, pairs)  42.6 us
    reshape x1, local copies, waits for them, and re-layouts, halving_scatter(): held = held.reshape((rows,) + (2,) * bits + (group,))  33.2 us
  transfers between devices with their start and end apart: 14, of which 6 were waited for; matrix products, arithmetic and copies ran while one was open for 5% of the time, Pallas kernels for 0%

profile of v1, /device:TPU:16, one launch (start us, length us, event | category | flops | bytes accessed | tf_op | source)
XLA Modules:
  0.0 1515.2 jit_solution(2068108656219526188)
XLA Ops:
  0.0 3.7 collective-permute-start.1
  3.7 3.4 collective-permute-start.2
  7.2 5.3 slice.8
  12.5 1.9 collective-permute-start
  14.4 6.5 collective-permute-start.5
  20.9 5.3 slice.9
  26.2 1.9 collective-permute-start.6
  28.1 0.7 neg.6
  28.8 0.1 copy.44
  28.9 0.8 sort.15
  29.7 0.1 copy.45
  29.8 0.1 fusion.9
  29.9 0.7 select_reduce_fusion
  30.7 0.1 select_reduce_fusion.1
  30.8 134.1 %collective-permute-done = bf16[160,1280]{1,0:T(8,128)(2,1)} collective-permute-done((bf16[160,1280]{1,0:T(8,128)(2,1)}, bf16[160,1280]{1,0:T(8,128)(2,1)}, u32[]{:S(2)}, u32[]{:S(2)}) %collective-permute-start) | collective-permute-done | bytes 409632 | tf_op jit(solution)/shard_map/ppermute | solution.py:21
  164.9 1.9 collective-permute-start.11
  166.8 0.1 subtract_select_fusion
  166.9 0.1 and.49
  167.0 0.1 reshape.196
  167.1 0.1 stack_reshape.9
  167.2 0.1 ne.74
  167.2 0.1 rem.55
  167.3 0.0 copy-start.1
  167.3 0.6 pad_add_fusion.rows_ref
  167.9 11.9 and_convert_fusion.keep_ref
  179.9 1.6 copy.53
  181.5 8.0 collective-permute-start.3
  189.5 1.6 copy.54
  191.1 4.6 collective-permute-start.7
  195.7 1.6 copy.55
  197.4 4.1 collective-permute-start.8
  201.5 1.6 copy.56
  203.1 2.5 fusion.7
  205.6 2.4 fusion.5
  208.0 1.9 collective-permute-start.4
  209.9 3.8 constant_dynamic-update-slice_fusion.4
  213.8 2.6 collective-permute-start.9
  216.4 3.8 constant_dynamic-update-slice_fusion.3
  220.2 1.9 constant_dynamic-update-slice_fusion.2
  222.1 35.7 %collective-permute-done.7 = bf16[1280,1280]{1,0:T(8,128)(2,1)S(1)} collective-permute-done((bf16[1280,1280]{1,0:T(8,128)(2,1)}, bf16[1280,1280]{1,0:T(8,128)(2,1)S(1)}, u32[]{:S(2)}, u32[]{:S(2)}) %collective-permute-start.7) | collective-permute-done | bytes 3276832 | tf_op jit(solution)/shard_map/ppermute | solution.py:21
  257.8 2.1 collective-permute-start.10
  259.9 1.9 constant_dynamic-update-slice_fusion.9
  261.8 71.5 %collective-permute-done.8 = bf16[1280,1280]{1,0:T(8,128)(2,1)S(1)} collective-permute-done((bf16[1280,1280]{1,0:T(8,128)(2,1)}, bf16[1280,1280]{1,0:T(8,128)(2,1)S(1)}, u32[]{:S(2)}, u32[]{:S(2)}) %collective-permute-start.8) | collective-permute-done | bytes 3276832 | tf_op jit(solution)/shard_map/ppermute | solution.py:21
  333.3 2.0 constant_dynamic-update-slice_fusion.8
  335.3 1.9 constant_dynamic-update-slice_fusion.7
  337.2 1.9 constant_dynamic-update-slice_fusion.1
  339.1 1.9 constant_dynamic-update-slice_fusion
  341.1 2.4 fusion.6.k_ref
  343.4 58.1 %collective-permute-done.9 = bf16[1280,1280]{1,0:T(8,128)(2,1)S(1)} collective-permute-done((bf16[1280,1280]{1,0:T(8,128)(2,1)S(1)}, bf16[1280,1280]{1,0:T(8,128)(2,1)S(1)}, u32[]{:S(2)}, u32[]{:S(2)}) %collective-permute-start.9) | collective-permute-done | bytes 3276832 | tf_op jit(solution)/shard_map/ppermute | solution.py:21
  401.5 1.9 constant_dynamic-update-slice_fusion.6
  403.4 60.5 %collective-permute-done.10 = bf16[1280,1280]{1,0:T(8,128)(2,1)S(1)} collective-permute-done((bf16[1280,1280]{1,0:T(8,128)(2,1)S(1)}, bf16[1280,1280]{1,0:T(8,128)(2,1)S(1)}, u32[]{:S(2)}, u32[]{:S(2)}) %collective-permute-start.10) | collective-permute-done | bytes 3276832 | tf_op jit(solution)/shard_map/ppermute | solution.py:21
  464.0 1.9 constant_dynamic-update-slice_fusion.5
  465.9 2.5 fusion.4.v_ref
  468.3 862.3 %shard_map.64 = bf16[1280,1280]{1,0:T(8,128)(2,1)} custom-call(s32[2,260]{1,0:T(2,128)} %pad_add_fusion.rows_ref, bf16[1280,1280]{1,0:T(8,128)(2,1)} %q_ref.1, bf16[8960,1280]{1,0:T(8,128)(2,1)} %fusion.6.k_ref, bf16[8960,1280]{1,0:T(8,128)(2,1)} %fusion.4.v_ref, f32[260,1,128]{2,1,0:T(1,128)} %and_convert_fusion.keep_ref), custom_call_target="tpu_custom_call" | custom-call | flops 21810380800 | bytes 176947200 | tf_op jit(solution)/shard_map/pallas_call | solution.py:94
  1330.6 23.4 %fusion = f32[1280,5120]{1,0:T(8,128)} fusion(bf16[1280,1280]{1,0:T(8,128)(2,1)} %shard_map.64, bf16[1280,5120]{1,0:T(8,128)(2,1)} %param.11), kind=kOutput, calls=%fused_computation.1 | convolution fusion | flops 16790323200 | bytes 42598400 | tf_op jit(solution)/shard_map/dot_general | solution.py:165
  1354.0 33.2 %reshape.198 = f32[1280,2,2,1280]{3,2,1,0:T(2,128)} reshape(f32[1280,5120]{1,0:T(8,128)} %fusion) | data formatting | bytes 52428800 | tf_op jit(solution)/shard_map/reshape | solution.py:124
  1387.2 14.6 constant_dynamic-slice_fusion
  1401.9 8.5 copy.61
  1410.4 13.1 constant_dynamic-slice_fusion.1
  1423.5 8.1 bitcast_add_fusion
  1431.5 4.9 fusion.3
  1436.4 1.5 collective-permute-start.13
  1437.9 72.0 %collective-permute-done.13 = bf16[1280,1280]{1,0:T(8,128)(2,1)S(1)} collective-permute-done((bf16[1280,1280]{1,0:T(8,128)(2,1)}, bf16[1280,1280]{1,0:T(8,128)(2,1)S(1)}, u32[]{:S(2)}, u32[]{:S(2)}) %collective-permute-start.13) | collective-permute-done | bytes 3276832 | tf_op jit(solution)/shard_map/ppermute | solution.py:131
  1509.9 5.3 fusion.2
  (16 shorter events, 0.1 us)
Async XLA Ops:
  0.0 208.0 %copy-start = (bf16[1280,1280]{1,0:T(8,128)(2,1)S(1)}, bf16[1280,1280]{1,0:T(8,128)(2,1)}, u32[]{:S(2)}) copy-start(bf16[1280,1280]{1,0:T(8,128)(2,1)} %param.7) | copy-start | bytes 9830404
  0.0 208.0 %collective-permute-start.1 = (bf16[1280,1280]{1,0:T(8,128)(2,1)}, bf16[1280,1280]{1,0:T(8,128)(2,1)}, u32[]{:S(2)}, u32[]{:S(2)}) collective-permute-start(bf16[1280,1280]{1,0:T(8,128)(2,1)} %param.7), channel_id=1, source_target_pairs={{0,8},{4,12},{8,16},{12,20},{16,24},{20,28},{1,9},{5,13},{9,17},{1... | collective-permute-start | bytes 9830408 | tf_op jit(solution)/shard_map/ppermute | solution.py:21
  3.7 210.0 %collective-permute-start.2 = (bf16[1280,1280]{1,0:T(8,128)(2,1)}, bf16[1280,1280]{1,0:T(8,128)(2,1)}, u32[]{:S(2)}, u32[]{:S(2)}) collective-permute-start(bf16[1280,1280]{1,0:T(8,128)(2,1)} %param.7), channel_id=1, source_target_pairs={{0,4},{4,8},{8,12},{12,16},{16,20},{20,24},{24,28},{1,5},{5,9},{9,... | collective-permute-start | bytes 9830408 | tf_op jit(solution)/shard_map/ppermute | solution.py:21
  12.5 152.4 %collective-permute-start = (bf16[160,1280]{1,0:T(8,128)(2,1)}, bf16[160,1280]{1,0:T(8,128)(2,1)}, u32[]{:S(2)}, u32[]{:S(2)}) collective-permute-start(bf16[160,1280]{1,0:T(8,128)(2,1)} %slice.8), channel_id=1, source_target_pairs={{0,12},{4,16},{8,20},{12,24},{16,28},{1,13},{5,17},{9,21},{13,25},... | collective-permute-start | bytes 1228808 | tf_op jit(solution)/shard_map/ppermute | solution.py:21
  14.4 167.1 %collective-permute-start.5 = (bf16[160,1280]{1,0:T(8,128)(2,1)}, bf16[160,1280]{1,0:T(8,128)(2,1)}, u32[]{:S(2)}, u32[]{:S(2)}) collective-permute-start(bf16[160,1280]{1,0:T(8,128)(2,1)} %slice.8), channel_id=1, source_target_pairs={{12,0},{16,4},{20,8},{24,12},{28,16},{13,1},{17,5},{21,9},{25,13},... | collective-permute-start | bytes 1228808 | tf_op jit(solution)/shard_map/ppermute | solution.py:21
  26.2 164.9 %collective-permute-start.6 = (bf16[160,1280]{1,0:T(8,128)(2,1)}, bf16[160,1280]{1,0:T(8,128)(2,1)}, u32[]{:S(2)}, u32[]{:S(2)}) collective-permute-start(bf16[160,1280]{1,0:T(8,128)(2,1)} %slice.9), channel_id=1, source_target_pairs={{0,12},{4,16},{8,20},{12,24},{16,28},{1,13},{5,17},{9,21},{13,25},... | collective-permute-start | bytes 1228808 | tf_op jit(solution)/shard_map/ppermute | solution.py:21
  164.9 32.5 %collective-permute-start.11 = (bf16[160,1280]{1,0:T(8,128)(2,1)}, bf16[160,1280]{1,0:T(8,128)(2,1)}, u32[]{:S(2)}, u32[]{:S(2)}) collective-permute-start(bf16[160,1280]{1,0:T(8,128)(2,1)} %slice.9), channel_id=1, source_target_pairs={{12,0},{16,4},{20,8},{24,12},{28,16},{13,1},{17,5},{21,9},{25,13},... | collective-permute-start | bytes 1228808 | tf_op jit(solution)/shard_map/ppermute | solution.py:21
  167.3 46.4 %copy-start.1 = (bf16[1280,1280]{1,0:T(8,128)(2,1)S(1)}, bf16[1280,1280]{1,0:T(8,128)(2,1)}, u32[]{:S(2)}) copy-start(bf16[1280,1280]{1,0:T(8,128)(2,1)} %param.8) | copy-start | bytes 9830404
  181.5 155.7 %collective-permute-start.3 = (bf16[1280,1280]{1,0:T(8,128)(2,1)}, bf16[1280,1280]{1,0:T(8,128)(2,1)S(1)}, u32[]{:S(2)}, u32[]{:S(2)}) collective-permute-start(bf16[1280,1280]{1,0:T(8,128)(2,1)} %param.7), channel_id=1, source_target_pairs={{4,0},{8,4},{12,8},{16,12},{20,16},{24,20},{28,24},{5,1},{9,5},{13... | collective-permute-start | bytes 9830408 | tf_op jit(solution)/shard_map/ppermute | solution.py:21
  191.1 66.6 %collective-permute-start.7 = (bf16[1280,1280]{1,0:T(8,128)(2,1)}, bf16[1280,1280]{1,0:T(8,128)(2,1)S(1)}, u32[]{:S(2)}, u32[]{:S(2)}) collective-permute-start(bf16[1280,1280]{1,0:T(8,128)(2,1)} %param.8), channel_id=1, source_target_pairs={{0,8},{4,12},{8,16},{12,20},{16,24},{20,28},{1,9},{5,13},{9,17},{1... | collective-permute-start | bytes 9830408 | tf_op jit(solution)/shard_map/ppermute | solution.py:21
  197.4 135.9 %collective-permute-start.8 = (bf16[1280,1280]{1,0:T(8,128)(2,1)}, bf16[1280,1280]{1,0:T(8,128)(2,1)S(1)}, u32[]{:S(2)}, u32[]{:S(2)}) collective-permute-start(bf16[1280,1280]{1,0:T(8,128)(2,1)} %param.8), channel_id=1, source_target_pairs={{0,4},{4,8},{8,12},{12,16},{16,20},{20,24},{24,28},{1,5},{5,9},{9,... | collective-permute-start | bytes 9830408 | tf_op jit(solution)/shard_map/ppermute | solution.py:21
  208.0 131.1 %collective-permute-start.4 = (bf16[1280,1280]{1,0:T(8,128)(2,1)S(1)}, bf16[1280,1280]{1,0:T(8,128)(2,1)S(1)}, u32[]{:S(2)}, u32[]{:S(2)}) collective-permute-start(bf16[1280,1280]{1,0:T(8,128)(2,1)S(1)} %copy-done), channel_id=1, source_target_pairs={{8,0},{12,4},{16,8},{20,12},{24,16},{28,20},{9,1},{13,5},{17,9},{2... | collective-permute-start | bytes 9830408 | tf_op jit(solution)/shard_map/ppermute | solution.py:21
  213.8 187.8 %collective-permute-start.9 = (bf16[1280,1280]{1,0:T(8,128)(2,1)S(1)}, bf16[1280,1280]{1,0:T(8,128)(2,1)S(1)}, u32[]{:S(2)}, u32[]{:S(2)}) collective-permute-start(bf16[1280,1280]{1,0:T(8,128)(2,1)S(1)} %copy-done.1), channel_id=1, source_target_pairs={{4,0},{8,4},{12,8},{16,12},{20,16},{24,20},{28,24},{5,1},{9,5},{13... | collective-permute-start | bytes 9830408 | tf_op jit(solution)/shard_map/ppermute | solution.py:21
  257.8 206.2 %collective-permute-start.10 = (bf16[1280,1280]{1,0:T(8,128)(2,1)S(1)}, bf16[1280,1280]{1,0:T(8,128)(2,1)S(1)}, u32[]{:S(2)}, u32[]{:S(2)}) collective-permute-start(bf16[1280,1280]{1,0:T(8,128)(2,1)S(1)} %copy-done.1), channel_id=1, source_target_pairs={{8,0},{12,4},{16,8},{20,12},{24,16},{28,20},{9,1},{13,5},{17,9},{2... | collective-permute-start | bytes 9830408 | tf_op jit(solution)/shard_map/ppermute | solution.py:21
  1410.4 13.1 collective-permute-start.12
  1436.4 73.5 %collective-permute-start.13 = (bf16[1280,1280]{1,0:T(8,128)(2,1)}, bf16[1280,1280]{1,0:T(8,128)(2,1)S(1)}, u32[]{:S(2)}, u32[]{:S(2)}) collective-permute-start(bf16[1280,1280]{1,0:T(8,128)(2,1)} %fusion.3), channel_id=1, source_target_pairs={{0,2},{1,3},{2,0},{3,1},{4,6},{5,7},{6,4},{7,5},{8,10},{9,11},{10,... | collective-permute-start | bytes 9830408 | tf_op jit(solution)/shard_map/ppermute | solution.py:131
